TPU v7x, 32 devices: a whole 2x2x4 slice. The times are simulated.
32 devices in a mesh: visit: 4 (over z), row: 2 (over core), col: 4 (over y, x).
Axes of the slice: x: 2, y: 2, z: 4, core: 2. Of those that a mesh axis runs over, the one named last changes fastest.
Arguments:
- images: bfloat16 [16, 1024, 2048], P('visit', 'row', 'col'), may hold values from -10 to 10, as said below
- coeffs: float32 [16, 3], P('visit'), may hold values from 0.3 to 1.2
- pair_list: int32 [8, 3], replicated, may hold values from 0 to 480, as said below
- weights: bfloat16 [16, 2, 4], P('visit', 'row', 'col'), may hold values from 0.5 to 4
- resample_bank: bfloat16 [12, 512, 512], replicated, may hold values from -0.25 to 0.25
- warp_index: int32 [16, 2, 4, 2], P('visit', 'row', 'col'), may hold values from 0 to 11
- destinations: int32 [16, 2, 4, 4], P('visit', 'row', 'col'), may hold values from 0 to 3, as said below
- counts: int32 [16, 2, 4], P('visit', 'row', 'col'), may hold values from 3 to 4
Outputs:
- coadd_patch: float32 [4, 1024, 2048], P('visit', 'row', 'col')
- plane_fit: float32 [16, 3], P('visit')
Inputs may be any that keep to these rules, and one draw needn't show every extreme that they name: `images`: noise plus a per-exposure sky plane. `pair_list`: every exposure appears in exactly one pair; offsets lie in 0 to 480, both ends used. `destinations`: the used entries of one tile's list are distinct; each tile lists the patch of its own visit index; a patch drawn with skew, which may be the device's own visit patch, is listed by all 4 tiles at each device position.
All inputs are finite; a program needn't handle non-finite values.
Results may differ from a plain program's by a relative error of at most 0.015.
Values may be sent and summed in bfloat16 or wider, within the bound.
No kernel may reach another device: no remote copies, remote signals or barrier semaphores. Data moves between devices by JAX's collectives and lax.ppermute only.
A program may use at most 192 MiB of HBM per device.

v0:
```python
import jax
import jax.numpy as jnp
from jax import lax
from jax.sharding import PartitionSpec as P

HALO = 16
STRIP = 32
MAXD = 4
SIGMA_PARTS = (0.0625, 0.125, 0.25)


def extended(value, sides, width):
    for axis, dim in sides:
        devices, length = (lax.axis_size(axis), value.shape[dim])
        up = [(i, (i + 1) % devices) for i in range(devices - 1)]
        down = [(j, i) for i, j in up]
        last = lax.slice_in_dim(value, length - width, length, axis=dim)
        initial = lax.slice_in_dim(value, 0, width, axis=dim)
        before = lax.ppermute(last, axis, up)
        after = lax.ppermute(initial, axis, down)
        value = jnp.concatenate([before, value, after], axis=dim)
    return value


def band_table(length, width, sigma):
    spread = (jnp.arange(2 * width + 1) - width).astype(jnp.float32)
    curve = jnp.exp(-spread * spread / (2.0 * sigma * sigma))
    total = jnp.sum(curve)
    rows_grid = lax.broadcasted_iota(jnp.int32, (length, length + 2 * width), 0)
    cols_grid = lax.broadcasted_iota(jnp.int32, (length, length + 2 * width), 1)
    offset = (cols_grid - rows_grid - width).astype(jnp.float32)
    values = jnp.exp(-offset * offset / (2.0 * sigma * sigma)) / total
    return jnp.where(jnp.abs(offset) <= width, values, 0.0).astype(jnp.bfloat16)


def centred(index, length):
    return (index.astype(jnp.float32) + 0.5) / length * 2.0 - 1.0


def solve_three(normal, moments):
    lower = jnp.linalg.cholesky(normal)
    first = moments[..., 0] / lower[..., 0, 0]
    second = (moments[..., 1] - lower[..., 1, 0] * first) / lower[..., 1, 1]
    third = (moments[..., 2] - lower[..., 2, 0] * first - lower[..., 2, 1] * second) / lower[
        ..., 2, 2
    ]
    upper_top = third / lower[..., 2, 2]
    upper_mid = (second - lower[..., 2, 1] * upper_top) / lower[..., 1, 1]
    upper_low = (first - lower[..., 1, 0] * upper_mid - lower[..., 2, 0] * upper_top) / lower[
        ..., 0, 0
    ]
    return jnp.stack([upper_low, upper_mid, upper_top], -1)


def rows_from(source, anchor):
    return lax.dynamic_slice_in_dim(source, anchor, STRIP, 0)


def shards(images, coeffs, pair_list, weights, resample_bank, warp_index, destinations, counts):
    exp_dev = images.shape[0]
    tile_len = images.shape[1]
    row_count = lax.axis_size("row")
    col_count = lax.axis_size("col")
    visit_count = lax.axis_size("visit")
    row_pos = lax.axis_index("row")
    col_pos = lax.axis_index("col")
    visit_pos = lax.axis_index("visit")
    height = row_count * tile_len
    breadth = col_count * tile_len
    padded = extended(images, (("row", 1), ("col", 2)), HALO)
    matched = jnp.zeros((exp_dev, tile_len, tile_len), jnp.float32)
    for kernel in range(len(SIGMA_PARTS)):
        table = band_table(tile_len, HALO, HALO * SIGMA_PARTS[kernel])
        across = jnp.einsum(
            "ij,ejl->eil", table, padded, preferred_element_type=jnp.float32
        ).astype(jnp.bfloat16)
        smoothed = jnp.einsum("eil,ml->eim", across, table, preferred_element_type=jnp.float32)
        matched = matched + coeffs[:, kernel, None, None] * smoothed
    own_ids = visit_pos * exp_dev + jnp.arange(exp_dev, dtype=jnp.int32)
    first_col = pair_list[:, 0]
    second_col = pair_list[:, 1]
    offsets = pair_list[:, 2]
    hit_first = first_col[None, :] == own_ids[:, None]
    hit_second = second_col[None, :] == own_ids[:, None]
    partner = jnp.sum(
        jnp.where(hit_first, second_col[None, :], 0) + jnp.where(hit_second, first_col[None, :], 0),
        axis=1,
    )
    offset = jnp.sum(jnp.where(hit_first | hit_second, offsets[None, :], 0), axis=1)
    own_strip = jax.vmap(rows_from)(images, offset)
    everyone = lax.all_gather(own_strip, "visit", axis=0, tiled=True)
    theirs = jnp.take(everyone, partner, axis=0).astype(jnp.float32)
    nearby = jax.vmap(rows_from)(matched, offset)
    difference = nearby - theirs
    pixel_weight = 1.0 / (1.0 + theirs * theirs)
    strip_rows = row_pos * tile_len + offset[:, None] + jnp.arange(STRIP, dtype=jnp.int32)[None, :]
    ycoord = centred(strip_rows, height)[:, :, None]
    xcoord = centred(col_pos * tile_len + jnp.arange(tile_len, dtype=jnp.int32), breadth)
    xgrid = xcoord[None, None, :]
    weight_x = pixel_weight * xgrid
    weight_y = pixel_weight * ycoord
    sum_w = jnp.sum(pixel_weight, axis=(1, 2))
    sum_x = jnp.sum(weight_x, axis=(1, 2))
    sum_y = jnp.sum(weight_y, axis=(1, 2))
    sum_xx = jnp.sum(weight_x * xgrid, axis=(1, 2))
    sum_xy = jnp.sum(weight_x * ycoord, axis=(1, 2))
    sum_yy = jnp.sum(weight_y * ycoord, axis=(1, 2))
    normal = jnp.stack(
        [
            jnp.stack([sum_w, sum_x, sum_y], -1),
            jnp.stack([sum_x, sum_xx, sum_xy], -1),
            jnp.stack([sum_y, sum_xy, sum_yy], -1),
        ],
        1,
    )
    moments = jnp.stack(
        [
            jnp.sum(pixel_weight * difference, axis=(1, 2)),
            jnp.sum(weight_x * difference, axis=(1, 2)),
            jnp.sum(weight_y * difference, axis=(1, 2)),
        ],
        -1,
    )
    normal, moments = lax.psum((normal, moments), ("row", "col"))
    plane_fit = solve_three(normal, moments)
    row_coord = centred(row_pos * tile_len + jnp.arange(tile_len, dtype=jnp.int32), height)
    background = (
        plane_fit[:, 0, None, None]
        + plane_fit[:, 1, None, None] * xcoord[None, None, :]
        + plane_fit[:, 2, None, None] * row_coord[None, :, None]
    )
    corrected = (matched - background).astype(jnp.bfloat16)
    choose = warp_index[:, 0, 0, :]
    row_maps = jnp.take(resample_bank, choose[:, 0], axis=0)
    col_maps = jnp.take(resample_bank, choose[:, 1], axis=0)
    halfway = jnp.einsum(
        "eij,ejk->eik", row_maps, corrected, preferred_element_type=jnp.float32
    ).astype(jnp.bfloat16)
    warped = jnp.einsum(
        "eik,elk->eil", halfway, col_maps, preferred_element_type=jnp.float32
    ).astype(jnp.bfloat16)
    listed = destinations[:, 0, 0, :]
    how_many = counts[:, 0, 0]
    usable = jnp.arange(MAXD, dtype=jnp.int32)[None, :] < how_many[:, None]
    owners = jnp.arange(visit_count, dtype=jnp.int32)
    member = jnp.any(usable[:, :, None] & (listed[:, :, None] == owners[None, None, :]), axis=1)
    tile_weight = weights[:, 0, 0]
    nothing = jnp.zeros((), jnp.bfloat16)
    picked = jnp.where(member, tile_weight[:, None], nothing)
    partial_sum = jnp.einsum("ev,eij->vij", picked, warped, preferred_element_type=jnp.float32)
    partial_weight = jnp.sum(picked.astype(jnp.float32), axis=0)
    numerator, denominator = (
        lax.psum_scatter(
            partial_sum.astype(jnp.bfloat16), "visit", scatter_dimension=0, tiled=True
        ).astype(jnp.float32),
        lax.psum_scatter(
            partial_weight.astype(jnp.bfloat16), "visit", scatter_dimension=0, tiled=True
        ).astype(jnp.float32),
    )
    coadd_patch = numerator / denominator[:, None, None]
    return (coadd_patch, plane_fit)


def solution(mesh):
    in_specs = (
        P("visit", "row", "col"),
        P("visit", None),
        P(),
        P("visit", "row", "col"),
        P(),
        P("visit", "row", "col", None),
        P("visit", "row", "col", None),
        P("visit", "row", "col"),
    )
    out_specs = (P("visit", "row", "col"), P("visit", None))
    return jax.shard_map(shards, mesh=mesh, in_specs=in_specs, out_specs=out_specs, check_vma=False)
```

profile of v0, /device:TPU:0, one launch (start us, length us, event | category | flops | bytes accessed | tf_op | source)
XLA Modules:
  0.0 194.2 jit_solution(17051824752516389986)
XLA Ops:
  9.1 2.4 %collective-permute-start = (bf16[4,16,512]{1,2,0:T(8,128)(2,1)}, bf16[4,16,512]{1,2,0:T(8,128)(2,1)S(1)}, u32[]{:S(2)}, u32[]{:S(2)}) collective-permute-start(bf16[4,16,512]{1,2,0:T(8,128)(2,1)} %copy.60), channel_id=1, source_target_pairs={{0,4},{1,5},{2,6},{3,7},{8,12},{9,13},{10,14},{11,15},{16,20},{17,... | collective-permute-start | bytes 196616 | tf_op jit(solution)/shard_map/ppermute | solution.py:19
  12.5 1.4 collective-permute-start.1
  13.9 4.2 %copy.62 = bf16[4,512,512]{1,2,0:T(8,128)(2,1)} copy(bf16[4,512,512]{2,1,0:T(8,128)(2,1)} %param.10) | data formatting | bytes 4194304 | tf_op args[0]
  19.9 2.9 %copy.63 = bf16[4,512,512]{2,0,1:T(4,128)(2,1)} copy(bf16[4,512,512]{2,1,0:T(8,128)(2,1)S(1)} %copy-done) | data formatting | bytes 4194304 | tf_op args[0]
  23.3 1.9 gather_fusion.1
  25.2 17.4 %all_gather.3 = bf16[16,32,512]{2,1,0:T(8,128)(2,1)S(1)} all-gather(bf16[4,32,512]{2,1,0:T(8,128)(2,1)S(1)} %copy.64), channel_id=1, replica_groups=mesh['visit'=4,'row'=2,'col'=4] {'visit'}, dimensions={0}, use_global_device_ids=true | all-gather | bytes 655360 | tf_op jit(solution)/shard_map/all_gather | solution.py:91
  42.7 4.8 %gather_fusion.3 = bf16[4,512,512]{2,1,0:T(8,128)(2,1)} fusion(bf16[12,512,512]{2,1,0:T(8,128)(2,1)} %param.14, s32[1024]{0:T(1024)S(1)} %get-tuple-element.65), kind=kCustom, calls=%fused_computation.clone | custom fusion | bytes 4194320 | tf_op jit(solution)/shard_map/jit(_take)/gather | solution.py:134
  47.5 5.0 %gather_fusion.4 = bf16[4,512,512]{2,1,0:T(8,128)(2,1)} fusion(bf16[12,512,512]{2,1,0:T(8,128)(2,1)} %param.14, s32[1024]{0:T(1024)S(1)} %get-tuple-element.64), kind=kCustom, calls=%fused_computation.1.clone | custom fusion | bytes 4194320 | tf_op jit(solution)/shard_map/jit(_take)/gather | solution.py:135
  54.1 3.4 %collective-permute-start.2 = (bf16[4,544,16]{1,2,0:T(8,128)(2,1)S(1)}, bf16[4,544,16]{1,2,0:T(8,128)(2,1)S(1)}, u32[]{:S(2)}, u32[]{:S(2)}) collective-permute-start(bf16[4,544,16]{1,2,0:T(8,128)(2,1)S(1)} %get-tuple-element.49), channel_id=1, source_target_pairs={{0,1},{1,2},{2,3},{4,5},{5,6},{6,7},{8,9},{9,10},{10,11},{12,13},{... | collective-permute-start | bytes 208904 | tf_op jit(solution)/shard_map/ppermute | solution.py:19
  57.5 1.5 collective-permute-start.3
  59.6 4.2 %collective-permute-done.3 = bf16[4,544,16]{1,2,0:T(8,128)(2,1)S(1)} collective-permute-done((bf16[4,544,16]{1,2,0:T(8,128)(2,1)S(1)}, bf16[4,544,16]{1,2,0:T(8,128)(2,1)S(1)}, u32[]{:S(2)}, u32[]{:S(2)}) %collective-permute-start.3) | collective-permute-done | bytes 69664 | tf_op jit(solution)/shard_map/ppermute | solution.py:20
  63.9 7.6 %fusion.2 = f32[4,512,512]{2,1,0:T(8,128)} fusion(f32[]{:T(128)} %exponential_reduce_fusion.1, bf16[4,544,16]{1,2,0:T(8,128)(2,1)S(1)} %collective-permute-done.3, bf16[4,16,512]{1,2,0:T(8,128)(2,1)} %collective-permute-done.1, bf16[4,512,512]{1,2,0:T(8,128)(2,1)S(1)} %copy-done.1, bf16[4,16,512]{1,2,0:T(8,128)(2,1)S(1)} %collective-permute-done, ...), kind=kOutput, calls=%fused_computation.10 | convolution fusion | flops 2372083712 | bytes 6561796 | tf_op jit(solution)/shard_map/eil,ml->eim/dot_general | solution.py:77
  71.4 7.7 %fusion = f32[4,512,512]{2,1,0:T(8,128)} fusion(f32[]{:T(128)} %exponential_reduce_fusion, bf16[4,544,16]{1,2,0:T(8,128)(2,1)S(1)} %collective-permute-done.3, bf16[4,16,512]{1,2,0:T(8,128)(2,1)} %collective-permute-done.1, bf16[4,512,512]{1,2,0:T(8,128)(2,1)S(1)} %copy-done.1, bf16[4,16,512]{1,2,0:T(8,128)(2,1)S(1)} %collective-permute-done, ...), kind=kOutput, calls=%fused_computation.8 | convolution fusion | flops 2372083712 | bytes 6561796 | tf_op jit(solution)/shard_map/eil,ml->eim/dot_general | solution.py:77
  79.1 9.8 %multiply_add_fusion = f32[4,512,512]{2,1,0:T(8,128)} fusion(f32[4,512,512]{2,1,0:T(8,128)} %fusion, f32[4,512,512]{2,1,0:T(8,128)} %fusion.2, f32[4]{0:T(128)S(1)} %get-tuple-element.30, f32[4]{0:T(128)S(1)} %get-tuple-element.31, f32[4]{0:T(128)S(1)} %get-tuple-element.29, f32[]{:T(128)} %exponential_reduce_fusion.2, ...), kind=kOutput, calls=%fused_computation.6 | convolution fusion | flops 2377326592 | bytes 14950452 | tf_op jit(solution)/shard_map/eil,ml->eim/dot_general | solution.py:77
  88.9 6.8 %copy.65 = f32[4,512,512]{2,0,1:T(4,128)} copy(f32[4,512,512]{2,1,0:T(8,128)} %multiply_add_fusion) | data formatting | bytes 8388608 | tf_op jit(solution)/shard_map/add | solution.py:78
  95.7 1.9 gather_fusion.2
  98.5 27.4 %all-reduce.2 = (f32[4,3,3]{1,2,0:T(4,128)S(1)}, f32[4,3]{0,1:T(4,128)S(1)}) all-reduce(f32[4,3,3]{1,2,0:T(4,128)S(1)} %pad_maximum_fusion.4, f32[4,3]{0,1:T(4,128)S(1)} %pad_maximum_fusion.5), channel_id=1, replica_groups=mesh['visit'=4,'row'=2,'col'=4] {'row','col'}, use_global_device_ids=true, to_apply=%region_16.18 | all-reduce | flops 48 | bytes 384 | tf_op jit(solution)/shard_map/psum | solution.py:124
  128.1 6.7 %fusion.22 = bf16[4,512,512]{2,1,0:T(8,128)(2,1)} fusion(bf16[4,512,512]{2,1,0:T(8,128)(2,1)} %gather_fusion.4, pred[4]{0:T(512)(128)(4,1)S(1)} %get-tuple-element.59, f32[4,512,512]{2,1,0:T(8,128)} %multiply_add_fusion, bf16[4,512,512]{2,1,0:T(8,128)(2,1)S(1)} %copy-done.2, f32[4,512]{1,0:T(4,128)S(1)} %get-tuple-element.67, ...), kind=kOutput, calls=%fused_computation.28 | convolution fusion | flops 2154823680 | bytes 10502152 | tf_op jit(solution)/shard_map/eik,elk->eil/dot_general | solution.py:139
  134.8 4.0 %fusion.27 = bf16[4,512,512]{2,0,1:T(4,128)(2,1)S(1)} fusion(bf16[4,512,512]{2,1,0:T(8,128)(2,1)} %fusion.22, pred[4,4]{1,0:T(4,128)(4,1)S(1)} %fusion.79, bf16[4]{0:T(256)(128)(2,1)S(1)} %bitcast.139), kind=kOutput, calls=%fused_computation.29 | convolution fusion | flops 9437200 | bytes 4194328 | tf_op jit(solution)/shard_map/ev,eij->vij/dot_general | solution.py:150
  138.8 1.8 copy.79
  140.7 11.5 %all-reduce.1 = bf16[4]{0:T(256)(128)(2,1)S(1)} all-reduce(bf16[4]{0:T(256)(128)(2,1)S(1)} %select_reduce_fusion.2), channel_id=3, replica_groups=mesh['visit'=4,'row'=2,'col'=4] {'visit'}, use_global_device_ids=true, to_apply=%region_21.23.clone | all-reduce | flops 4 | bytes 16
  152.8 1.2 dynamic-slice.1
  155.4 29.8 %reduce-scatter.2.cloned.1.call-done = bf16[1,512,512]{2,1,0:T(8,128)(2,1)} async-done(((bf16[4,512,512]{2,1,0:T(8,128)(2,1)}), bf16[1,512,512]{2,1,0:T(8,128)(2,1)}) %reduce-scatter.2.cloned.1.call-update) | async-done | bytes 524304 | tf_op jit(solution)/shard_map/reduce_scatter | solution.py:153
  185.2 2.2 %convert_divide_fusion = f32[1,512,512]{2,1,0:T(8,128)} fusion(bf16[1,512,512]{2,1,0:T(8,128)(2,1)} %reduce-scatter.2.cloned.1.call-done, f32[]{:T(128)S(6)} %convert.2), kind=kLoop, calls=%fused_computation.40 | loop fusion | flops 524288 | bytes 1572868 | tf_op jit(solution)/shard_map/div | solution.py:160
  (79 shorter events, 12.0 us)
Async XLA Ops:
  7.2 178.1 %reduce-scatter.2.cloned.1.call-start = ((), (), s32[]{:S(2)}) async-start(), calls=%async_computation.1 | async-start | bytes 2621440 | tf_op jit(solution)/shard_map/reduce_scatter | solution.py:153
  9.1 44.1 %collective-permute-start = (bf16[4,16,512]{1,2,0:T(8,128)(2,1)}, bf16[4,16,512]{1,2,0:T(8,128)(2,1)S(1)}, u32[]{:S(2)}, u32[]{:S(2)}) collective-permute-start(bf16[4,16,512]{1,2,0:T(8,128)(2,1)} %copy.60), channel_id=1, source_target_pairs={{0,4},{1,5},{2,6},{3,7},{8,12},{9,13},{10,14},{11,15},{16,20},{17,... | collective-permute-start | bytes 196616 | tf_op jit(solution)/shard_map/ppermute | solution.py:19
  12.5 7.4 %copy-start = (bf16[4,512,512]{2,1,0:T(8,128)(2,1)S(1)}, bf16[4,512,512]{2,1,0:T(8,128)(2,1)}, u32[]{:S(2)}) copy-start(bf16[4,512,512]{2,1,0:T(8,128)(2,1)} %param.10) | copy-start | bytes 6291460
  12.5 40.7 %collective-permute-start.1 = (bf16[4,16,512]{1,2,0:T(8,128)(2,1)}, bf16[4,16,512]{1,2,0:T(8,128)(2,1)}, u32[]{:S(2)}, u32[]{:S(2)}) collective-permute-start(bf16[4,16,512]{1,2,0:T(8,128)(2,1)} %copy.61), channel_id=1, source_target_pairs={{4,0},{5,1},{6,2},{7,3},{12,8},{13,9},{14,10},{15,11},{20,16},{21,... | collective-permute-start | bytes 196616 | tf_op jit(solution)/shard_map/ppermute | solution.py:20
  19.9 2.9 %copy-start.5 = (s32[8,3]{0,1:T(4,128)S(1)}, s32[8,3]{0,1:T(4,128)}, u32[]{:S(2)}) copy-start(s32[8,3]{0,1:T(4,128)} %param.12) | copy-start | bytes 292
  19.9 3.2 %copy-start.3 = (f32[4,3]{1,0:T(4,128)S(1)}, f32[4,3]{1,0:T(4,128)}, u32[]{:S(2)}) copy-start(f32[4,3]{1,0:T(4,128)} %param.11) | copy-start | bytes 148
  22.8 19.8 %copy-start.6 = (s32[4,1,1,2]{0,3,2,1:T(2,128)S(1)}, s32[4,1,1,2]{0,3,2,1:T(2,128)}, u32[]{:S(2)}) copy-start(s32[4,1,1,2]{0,3,2,1:T(2,128)} %param.15) | copy-start | bytes 100
  47.5 5.0 %copy-start.7 = (s32[4,1,1]{0,2,1:T(1,128)S(1)}, s32[4,1,1]{0,2,1:T(1,128)}, u32[]{:S(2)}) copy-start(s32[4,1,1]{0,2,1:T(1,128)} %param.17) | copy-start | bytes 52
  47.5 5.6 %copy-start.4 = (s32[4,1,1,4]{3,2,1,0:T(1,128)S(1)}, s32[4,1,1,4]{3,2,1,0:T(1,128)}, u32[]{:S(2)}) copy-start(s32[4,1,1,4]{3,2,1,0:T(1,128)} %param.16) | copy-start | bytes 196
  47.5 5.8 %copy-start.1 = (bf16[4,512,512]{1,2,0:T(8,128)(2,1)S(1)}, bf16[4,512,512]{1,2,0:T(8,128)(2,1)}, u32[]{:S(2)}) copy-start(bf16[4,512,512]{1,2,0:T(8,128)(2,1)} %copy.62) | copy-start | bytes 6291460
  54.1 5.5 %collective-permute-start.2 = (bf16[4,544,16]{1,2,0:T(8,128)(2,1)S(1)}, bf16[4,544,16]{1,2,0:T(8,128)(2,1)S(1)}, u32[]{:S(2)}, u32[]{:S(2)}) collective-permute-start(bf16[4,544,16]{1,2,0:T(8,128)(2,1)S(1)} %get-tuple-element.49), channel_id=1, source_target_pairs={{0,1},{1,2},{2,3},{4,5},{5,6},{6,7},{8,9},{9,10},{10,11},{12,13},{... | collective-permute-start | bytes 208904 | tf_op jit(solution)/shard_map/ppermute | solution.py:19
  57.5 6.3 %collective-permute-start.3 = (bf16[4,544,16]{1,2,0:T(8,128)(2,1)S(1)}, bf16[4,544,16]{1,2,0:T(8,128)(2,1)S(1)}, u32[]{:S(2)}, u32[]{:S(2)}) collective-permute-start(bf16[4,544,16]{1,2,0:T(8,128)(2,1)S(1)} %get-tuple-element.50), channel_id=1, source_target_pairs={{1,0},{2,1},{3,2},{5,4},{6,5},{7,6},{9,8},{10,9},{11,10},{13,12},{... | collective-permute-start | bytes 208904 | tf_op jit(solution)/shard_map/ppermute | solution.py:20
  95.7 32.4 %copy-start.2 = (bf16[4,512,512]{2,1,0:T(8,128)(2,1)S(1)}, bf16[4,512,512]{2,1,0:T(8,128)(2,1)}, u32[]{:S(2)}) copy-start(bf16[4,512,512]{2,1,0:T(8,128)(2,1)} %gather_fusion.3) | copy-start | bytes 6291460
  128.1 6.7 %copy-start.8 = (bf16[4,1,1]{0,2,1:T(2,128)(2,1)S(1)}, bf16[4,1,1]{0,2,1:T(2,128)(2,1)}, u32[]{:S(2)}) copy-start(bf16[4,1,1]{0,2,1:T(2,128)(2,1)} %param.13) | copy-start | bytes 28
  140.6 11.6 %copy-start.9 = (u32[32]{0:T(128)S(1)}, u32[32]{0:T(128)}, u32[]{:S(2)}) copy-start(u32[32]{0:T(128)} %constant.184) | copy-start | bytes 388
Sparse Core Ops, SparseCore 0:
  140.7 44.4 reduce-scatter.1
where the time goes:
time: 195 us; the launch traced here: 194 us
  blocking collectives  56.3 us (29%)
  local copies, waits for them, and re-layouts  36.1 us (19%)
  matrix products  35.7 us (18%)
  waiting for transfers between devices  34.7 us (18%)
  between operations  14.9 us (8%)
  starting transfers between devices  8.7 us (4%)
  other arithmetic  7.86 us (4%)
    reduce_scatter x1, waiting for transfers between devices, shards(): lax.psum_scatter(partial_sum.astype(jnp.bfloat16), 'visit', scatter_dimen...  29.8 us
    psum x1, blocking collectives, shards(): normal, moments = lax.psum((normal, moments), ('row', 'col'))  27.4 us
    dot_general x3, matrix products, shards(): jnp.einsum('eil,ml->eim', across, table, preferred_element_type=jnp.float32)  25 us
    all_gather x1, blocking collectives, shards(): everyone = lax.all_gather(own_strip, 'visit', axis=0, tiled=True)  17.4 us
    unnamed x1, blocking collectives  11.5 us
    unnamed x25, local copies, waits for them, and re-layouts  9.58 us
    add x1, local copies, waits for them, and re-layouts, shards(): matched = matched + coeffs[:, kernel, None, None] * smoothed  6.81 us
    dot_general x1, matrix products, shards(): jnp.einsum('eik,elk->eil', halfway, col_maps, preferred_element_type=jnp....  6.68 us
  transfers between devices with their start and end apart: 5, of which 3 were waited for; matrix products, arithmetic and copies ran while one was open for 13% of the time, Pallas kernels for 0%

commit v1 on v0

--- a/solution.py
+++ b/solution.py
@@ -7,6 +7,23 @@
 STRIP = 32
 MAXD = 4
 SIGMA_PARTS = (0.0625, 0.125, 0.25)
+
+
+def in_order(blocks, dim):
+    dims = list(blocks.shape[1:])
+    dims[dim] *= blocks.shape[0]
+    return jnp.moveaxis(blocks, 0, dim).reshape(dims)
+
+
+def collect(value, axis, dim):
+    peers = lax.axis_size(axis)
+    right = [(i, (i + 1) % peers) for i in range(peers)]
+    tiles = [value]
+    while len(tiles) < peers:
+        tiles.append(lax.ppermute(tiles[-1], axis, right))
+    position = lax.axis_index(axis)
+    tiles = jnp.stack(tiles)[(position - jnp.arange(peers)) % peers]
+    return in_order(tiles, dim)
 
 
 def extended(value, sides, width):
@@ -88,7 +105,7 @@
     )
     offset = jnp.sum(jnp.where(hit_first | hit_second, offsets[None, :], 0), axis=1)
     own_strip = jax.vmap(rows_from)(images, offset)
-    everyone = lax.all_gather(own_strip, "visit", axis=0, tiled=True)
+    everyone = collect(own_strip, "visit", 0)
     theirs = jnp.take(everyone, partner, axis=0).astype(jnp.float32)
     nearby = jax.vmap(rows_from)(matched, offset)
     difference = nearby - theirs

time: 195 us -> 188 us (0.964)
  blocking collectives: 56.3 us -> 38.1 us
  other arithmetic: 7.86 us -> 13.8 us
  starting transfers between devices: 8.7 us -> 14.2 us
  waiting for transfers between devices: 34.7 us -> 32.6 us
  local copies, waits for them, and re-layouts: 36.1 us -> 38.1 us
    all_gather x1 -> x0, blocking collectives: 17.4 us -> none  [shards(): everyone = lax.all_gather(own_strip, 'visit', axis=0, tiled=True)]
    ppermute x0 -> x3, starting transfers between devices: none -> 5.83 us  [collect(): tiles.append(lax.ppermute(tiles[-1], axis, right))]
    unnamed x25 -> x37, local copies, waits for them, and re-layouts: 9.58 us -> 10.3 us
  transfers between devices with their start and end apart: 5 -> 8, of which waited for: 3 -> 2; matrix products, arithmetic and copies ran while one was open for 13% -> 33% of each run, Pallas kernels for 0% -> 0%
where the time goes in v1:
time: 188 us; the launch traced here: 187 us
  local copies, waits for them, and re-layouts  38.1 us (20%)
  blocking collectives  38.1 us (20%)
  matrix products  35.3 us (19%)
  waiting for transfers between devices  32.6 us (17%)
  between operations  14.9 us (8%)
  starting transfers between devices  14.2 us (8%)
  other arithmetic  13.8 us (7%)
    reduce_scatter x1, waiting for transfers between devices, shards(): lax.psum_scatter(partial_sum.astype(jnp.bfloat16), 'visit', scatter_dimen...  29.8 us
    psum x1, blocking collectives, shards(): normal, moments = lax.psum((normal, moments), ('row', 'col'))  27.4 us
    dot_general x3, matrix products, shards(): jnp.einsum('eil,ml->eim', across, table, preferred_element_type=jnp.float32)  24.6 us
    unnamed x1, blocking collectives  10.7 us
    unnamed x37, local copies, waits for them, and re-layouts  10.3 us
    add x1, local copies, waits for them, and re-layouts, shards(): matched = matched + coeffs[:, kernel, None, None] * smoothed  6.81 us
    dot_general x1, matrix products, shards(): jnp.einsum('eik,elk->eil', halfway, col_maps, preferred_element_type=jnp....  6.69 us
    ppermute x3, starting transfers between devices, collect(): tiles.append(lax.ppermute(tiles[-1], axis, right))  5.83 us
  transfers between devices with their start and end apart: 8, of which 2 were waited for; matrix products, arithmetic and copies ran while one was open for 33% of the time, Pallas kernels for 0%

profile of v1, /device:TPU:0, one launch (start us, length us, event | category | flops | bytes accessed | tf_op | source)
XLA Modules:
  0.0 187.0 jit_solution(12398171341446810850)
XLA Ops:
  9.1 2.4 %collective-permute-start = (bf16[4,16,512]{1,2,0:T(8,128)(2,1)}, bf16[4,16,512]{1,2,0:T(8,128)(2,1)S(1)}, u32[]{:S(2)}, u32[]{:S(2)}) collective-permute-start(bf16[4,16,512]{1,2,0:T(8,128)(2,1)} %copy.60), channel_id=1, source_target_pairs={{0,4},{1,5},{2,6},{3,7},{8,12},{9,13},{10,14},{11,15},{16,20},{17,... | collective-permute-start | bytes 196616 | tf_op jit(solution)/shard_map/ppermute | solution.py:36
  13.8 4.7 %copy.63 = bf16[4,512,512]{2,0,1:T(4,128)(2,1)} copy(bf16[4,512,512]{2,1,0:T(8,128)(2,1)} %param.10) | data formatting | bytes 4194304 | tf_op args[0]
  18.7 1.9 gather_fusion.2
  20.6 2.5 %collective-permute-start.4 = (bf16[4,32,512]{2,0,1:T(4,128)(2,1)S(1)}, bf16[4,32,512]{2,0,1:T(4,128)(2,1)S(1)}, u32[]{:S(2)}, u32[]{:S(2)}) collective-permute-start(bf16[4,32,512]{2,0,1:T(4,128)(2,1)S(1)} %gather_fusion.2), channel_id=1, source_target_pairs={{0,8},{8,16},{16,24},{24,0},{1,9},{9,17},{17,25},{25,1},{2,10},{10... | collective-permute-start | bytes 393224 | tf_op jit(solution)/shard_map/ppermute | solution.py:23
  23.1 2.4 %copy.62 = bf16[4,512,512]{1,2,0:T(8,128)(2,1)} copy(bf16[4,512,512]{2,1,0:T(8,128)(2,1)S(1)} %copy-done) | data formatting | bytes 4194304 | tf_op args[0]
  30.0 4.8 %gather_fusion.4 = bf16[4,512,512]{2,1,0:T(8,128)(2,1)} fusion(bf16[12,512,512]{2,1,0:T(8,128)(2,1)} %param.14, s32[1024]{0:T(1024)S(1)} %get-tuple-element.65), kind=kCustom, calls=%fused_computation.clone | custom fusion | bytes 4194320 | tf_op jit(solution)/shard_map/jit(_take)/gather | solution.py:151
  34.7 5.0 %gather_fusion.5 = bf16[4,512,512]{2,1,0:T(8,128)(2,1)} fusion(bf16[12,512,512]{2,1,0:T(8,128)(2,1)} %param.14, s32[1024]{0:T(1024)S(1)} %get-tuple-element.64), kind=kCustom, calls=%fused_computation.1.clone | custom fusion | bytes 4194320 | tf_op jit(solution)/shard_map/jit(_take)/gather | solution.py:152
  41.1 3.4 %collective-permute-start.2 = (bf16[4,544,16]{1,2,0:T(8,128)(2,1)S(1)}, bf16[4,544,16]{1,2,0:T(8,128)(2,1)S(1)}, u32[]{:S(2)}, u32[]{:S(2)}) collective-permute-start(bf16[4,544,16]{1,2,0:T(8,128)(2,1)S(1)} %get-tuple-element.49), channel_id=1, source_target_pairs={{0,1},{1,2},{2,3},{4,5},{5,6},{6,7},{8,9},{9,10},{10,11},{12,13},{... | collective-permute-start | bytes 208904 | tf_op jit(solution)/shard_map/ppermute | solution.py:36
  46.4 1.7 collective-permute-start.5
  48.7 2.8 %collective-permute-done.3 = bf16[4,544,16]{1,2,0:T(8,128)(2,1)} collective-permute-done((bf16[4,544,16]{1,2,0:T(8,128)(2,1)S(1)}, bf16[4,544,16]{1,2,0:T(8,128)(2,1)}, u32[]{:S(2)}, u32[]{:S(2)}) %collective-permute-start.3) | collective-permute-done | bytes 69664 | tf_op jit(solution)/shard_map/ppermute | solution.py:37
  51.5 7.6 %fusion.2 = f32[4,512,512]{2,1,0:T(8,128)} fusion(f32[]{:T(128)} %exponential_reduce_fusion.1, bf16[4,544,16]{1,2,0:T(8,128)(2,1)} %collective-permute-done.3, bf16[4,16,512]{1,2,0:T(8,128)(2,1)S(1)} %collective-permute-done.1, bf16[4,512,512]{1,2,0:T(8,128)(2,1)S(1)} %copy-done.1, bf16[4,16,512]{1,2,0:T(8,128)(2,1)S(1)} %collective-permute-done, ...), kind=kOutput, calls=%fused_computation.11 | convolution fusion | flops 2372083712 | bytes 6561796 | tf_op jit(solution)/shard_map/eil,ml->eim/dot_general | solution.py:94
  59.1 7.5 %fusion = f32[4,512,512]{2,1,0:T(8,128)} fusion(f32[]{:T(128)} %exponential_reduce_fusion, bf16[4,544,16]{1,2,0:T(8,128)(2,1)} %collective-permute-done.3, bf16[4,16,512]{1,2,0:T(8,128)(2,1)S(1)} %collective-permute-done.1, bf16[4,512,512]{1,2,0:T(8,128)(2,1)S(1)} %copy-done.1, bf16[4,16,512]{1,2,0:T(8,128)(2,1)S(1)} %collective-permute-done, ...), kind=kOutput, calls=%fused_computation.9 | convolution fusion | flops 2372083712 | bytes 6561796 | tf_op jit(solution)/shard_map/eil,ml->eim/dot_general | solution.py:94
  66.6 1.7 collective-permute-start.6
  68.3 9.5 %multiply_add_fusion = f32[4,512,512]{2,1,0:T(8,128)} fusion(f32[4,512,512]{2,1,0:T(8,128)} %fusion, f32[4,512,512]{2,1,0:T(8,128)} %fusion.2, f32[4]{0:T(128)S(1)} %get-tuple-element.30, f32[4]{0:T(128)S(1)} %get-tuple-element.31, f32[4]{0:T(128)S(1)} %get-tuple-element.29, f32[]{:T(128)} %exponential_reduce_fusion.2, ...), kind=kOutput, calls=%fused_computation.7 | convolution fusion | flops 2377326592 | bytes 14950452 | tf_op jit(solution)/shard_map/eil,ml->eim/dot_general | solution.py:94
  77.8 6.8 %copy.65 = f32[4,512,512]{2,0,1:T(4,128)} copy(f32[4,512,512]{2,1,0:T(8,128)} %multiply_add_fusion) | data formatting | bytes 8388608 | tf_op jit(solution)/shard_map/add | solution.py:95
  84.6 1.9 %gather_fusion.3 = f32[4,32,512]{2,0,1:T(4,128)S(1)} fusion(f32[4,512,512]{2,0,1:T(4,128)} %copy.65, s32[4]{0:T(128)S(1)} %fusion.97), kind=kCustom, calls=%fused_computation.5 | custom fusion | bytes 524336 | tf_op jit(solution)/shard_map/vmap()/gather | solution.py:73
  86.5 1.6 pad_maximum_fusion.1
  90.9 27.4 %all-reduce.2 = (f32[4,3,3]{1,2,0:T(4,128)S(1)}, f32[4,3]{0,1:T(4,128)S(1)}) all-reduce(f32[4,3,3]{1,2,0:T(4,128)S(1)} %pad_maximum_fusion.5, f32[4,3]{0,1:T(4,128)S(1)} %pad_maximum_fusion.6), channel_id=1, replica_groups=mesh['visit'=4,'row'=2,'col'=4] {'row','col'}, use_global_device_ids=true, to_apply=%region_16.18 | all-reduce | flops 48 | bytes 384 | tf_op jit(solution)/shard_map/psum | solution.py:141
  121.8 6.7 %fusion.22 = bf16[4,512,512]{2,1,0:T(8,128)(2,1)} fusion(bf16[4,512,512]{2,1,0:T(8,128)(2,1)} %gather_fusion.5, pred[4]{0:T(512)(128)(4,1)} %get-tuple-element.59, f32[4,512,512]{2,1,0:T(8,128)} %multiply_add_fusion, bf16[4,512,512]{2,1,0:T(8,128)(2,1)S(1)} %copy-done.2, f32[4,512]{1,0:T(4,128)S(1)} %get-tuple-element.67, ...), kind=kOutput, calls=%fused_computation.29 | convolution fusion | flops 2154823680 | bytes 10502152 | tf_op jit(solution)/shard_map/eik,elk->eil/dot_general | solution.py:156
  128.5 4.0 %fusion.27 = bf16[4,512,512]{2,0,1:T(4,128)(2,1)S(1)} fusion(bf16[4,512,512]{2,1,0:T(8,128)(2,1)} %fusion.22, pred[4,4]{1,0:T(4,128)(4,1)S(1)} %copy-done.10, bf16[4]{0:T(256)(128)(2,1)S(1)} %bitcast.149), kind=kOutput, calls=%fused_computation.30 | convolution fusion | flops 9437200 | bytes 4194328 | tf_op jit(solution)/shard_map/ev,eij->vij/dot_general | solution.py:167
  132.5 1.8 copy.79
  134.3 10.7 %all-reduce.1 = bf16[4]{0:T(256)(128)(2,1)S(1)} all-reduce(bf16[4]{0:T(256)(128)(2,1)S(1)} %select_reduce_fusion.2), channel_id=3, replica_groups=mesh['visit'=4,'row'=2,'col'=4] {'visit'}, use_global_device_ids=true, to_apply=%region_21.23.clone | all-reduce | flops 4 | bytes 16
  148.2 29.8 %reduce-scatter.2.cloned.1.call-done = bf16[1,512,512]{2,1,0:T(8,128)(2,1)} async-done(((bf16[4,512,512]{2,1,0:T(8,128)(2,1)}), bf16[1,512,512]{2,1,0:T(8,128)(2,1)}) %reduce-scatter.2.cloned.1.call-update) | async-done | bytes 524304 | tf_op jit(solution)/shard_map/reduce_scatter | solution.py:170
  178.0 2.2 %convert_divide_fusion = f32[1,512,512]{2,1,0:T(8,128)} fusion(bf16[1,512,512]{2,1,0:T(8,128)(2,1)} %reduce-scatter.2.cloned.1.call-done, f32[]{:T(128)S(6)} %convert.2), kind=kLoop, calls=%fused_computation.41 | loop fusion | flops 524288 | bytes 1572868 | tf_op jit(solution)/shard_map/div | solution.py:177
  (100 shorter events, 21.6 us)
Async XLA Ops:
  7.2 170.9 %reduce-scatter.2.cloned.1.call-start = ((), (), s32[]{:S(2)}) async-start(), calls=%async_computation.1 | async-start | bytes 2621440 | tf_op jit(solution)/shard_map/reduce_scatter | solution.py:170
  9.1 31.9 %collective-permute-start = (bf16[4,16,512]{1,2,0:T(8,128)(2,1)}, bf16[4,16,512]{1,2,0:T(8,128)(2,1)S(1)}, u32[]{:S(2)}, u32[]{:S(2)}) collective-permute-start(bf16[4,16,512]{1,2,0:T(8,128)(2,1)} %copy.60), channel_id=1, source_target_pairs={{0,4},{1,5},{2,6},{3,7},{8,12},{9,13},{10,14},{11,15},{16,20},{17,... | collective-permute-start | bytes 196616 | tf_op jit(solution)/shard_map/ppermute | solution.py:36
  12.5 28.5 %collective-permute-start.1 = (bf16[4,16,512]{1,2,0:T(8,128)(2,1)}, bf16[4,16,512]{1,2,0:T(8,128)(2,1)S(1)}, u32[]{:S(2)}, u32[]{:S(2)}) collective-permute-start(bf16[4,16,512]{1,2,0:T(8,128)(2,1)} %copy.61), channel_id=1, source_target_pairs={{4,0},{5,1},{6,2},{7,3},{12,8},{13,9},{14,10},{15,11},{20,16},{21,... | collective-permute-start | bytes 196616 | tf_op jit(solution)/shard_map/ppermute | solution.py:37
  13.8 4.7 %copy-start.7 = (s32[8,3]{0,1:T(4,128)S(1)}, s32[8,3]{0,1:T(4,128)}, u32[]{:S(2)}) copy-start(s32[8,3]{0,1:T(4,128)} %param.12) | copy-start | bytes 292
  13.8 9.3 %copy-start = (bf16[4,512,512]{2,1,0:T(8,128)(2,1)S(1)}, bf16[4,512,512]{2,1,0:T(8,128)(2,1)}, u32[]{:S(2)}) copy-start(bf16[4,512,512]{2,1,0:T(8,128)(2,1)} %param.10) | copy-start | bytes 6291460
  20.6 7.4 %copy-start.5 = (f32[4,3]{1,0:T(4,128)S(1)}, f32[4,3]{1,0:T(4,128)}, u32[]{:S(2)}) copy-start(f32[4,3]{1,0:T(4,128)} %param.11) | copy-start | bytes 148
  20.6 8.8 %copy-start.8 = (s32[4,1,1,2]{0,3,2,1:T(2,128)S(1)}, s32[4,1,1,2]{0,3,2,1:T(2,128)}, u32[]{:S(2)}) copy-start(s32[4,1,1,2]{0,3,2,1:T(2,128)} %param.15) | copy-start | bytes 100
  20.6 25.7 %collective-permute-start.4 = (bf16[4,32,512]{2,0,1:T(4,128)(2,1)S(1)}, bf16[4,32,512]{2,0,1:T(4,128)(2,1)S(1)}, u32[]{:S(2)}, u32[]{:S(2)}) collective-permute-start(bf16[4,32,512]{2,0,1:T(4,128)(2,1)S(1)} %gather_fusion.2), channel_id=1, source_target_pairs={{0,8},{8,16},{16,24},{24,0},{1,9},{9,17},{17,25},{25,1},{2,10},{10... | collective-permute-start | bytes 393224 | tf_op jit(solution)/shard_map/ppermute | solution.py:23
  34.7 5.0 %copy-start.13 = (s32[4,1,1]{0,2,1:T(1,128)S(1)}, s32[4,1,1]{0,2,1:T(1,128)}, u32[]{:S(2)}) copy-start(s32[4,1,1]{0,2,1:T(1,128)} %param.17) | copy-start | bytes 52
  34.7 5.1 %copy-start.6 = (s32[4,1,1,4]{3,2,1,0:T(1,128)S(1)}, s32[4,1,1,4]{3,2,1,0:T(1,128)}, u32[]{:S(2)}) copy-start(s32[4,1,1,4]{3,2,1,0:T(1,128)} %param.16) | copy-start | bytes 196
  34.7 6.3 %copy-start.1 = (bf16[4,512,512]{1,2,0:T(8,128)(2,1)S(1)}, bf16[4,512,512]{1,2,0:T(8,128)(2,1)}, u32[]{:S(2)}) copy-start(bf16[4,512,512]{1,2,0:T(8,128)(2,1)} %copy.62) | copy-start | bytes 6291460
  41.1 6.9 %collective-permute-start.2 = (bf16[4,544,16]{1,2,0:T(8,128)(2,1)S(1)}, bf16[4,544,16]{1,2,0:T(8,128)(2,1)S(1)}, u32[]{:S(2)}, u32[]{:S(2)}) collective-permute-start(bf16[4,544,16]{1,2,0:T(8,128)(2,1)S(1)} %get-tuple-element.49), channel_id=1, source_target_pairs={{0,1},{1,2},{2,3},{4,5},{5,6},{6,7},{8,9},{9,10},{10,11},{12,13},{... | collective-permute-start | bytes 208904 | tf_op jit(solution)/shard_map/ppermute | solution.py:36
  44.6 6.9 %collective-permute-start.3 = (bf16[4,544,16]{1,2,0:T(8,128)(2,1)S(1)}, bf16[4,544,16]{1,2,0:T(8,128)(2,1)}, u32[]{:S(2)}, u32[]{:S(2)}) collective-permute-start(bf16[4,544,16]{1,2,0:T(8,128)(2,1)S(1)} %get-tuple-element.50), channel_id=1, source_target_pairs={{1,0},{2,1},{3,2},{5,4},{6,5},{7,6},{9,8},{10,9},{11,10},{13,12},{... | collective-permute-start | bytes 208904 | tf_op jit(solution)/shard_map/ppermute | solution.py:37
  46.4 12.7 %copy-start.3 = (bf16[4,32,512]{2,0,1:T(4,128)(2,1)}, bf16[4,32,512]{2,0,1:T(4,128)(2,1)S(1)}, u32[]{:S(2)}) copy-start(bf16[4,32,512]{2,0,1:T(4,128)(2,1)S(1)} %collective-permute-done.4) | copy-start | bytes 393220
  46.4 20.2 %collective-permute-start.5 = (bf16[4,32,512]{2,0,1:T(4,128)(2,1)S(1)}, bf16[4,32,512]{2,0,1:T(4,128)(2,1)}, u32[]{:S(2)}, u32[]{:S(2)}) collective-permute-start(bf16[4,32,512]{2,0,1:T(4,128)(2,1)S(1)} %collective-permute-done.4), channel_id=1, source_target_pairs={{0,8},{8,16},{16,24},{24,0},{1,9},{9,17},{17,25},{25,1},{2,10},{10... | collective-permute-start | bytes 393224 | tf_op jit(solution)/shard_map/ppermute | solution.py:23
  48.1 0.6 copy-start.11
  51.5 7.6 %copy-start.12 = (bf16[4,544,16]{1,2,0:T(8,128)(2,1)S(1)}, bf16[4,544,16]{1,2,0:T(8,128)(2,1)}, u32[]{:S(2)}) copy-start(bf16[4,544,16]{1,2,0:T(8,128)(2,1)} %copy-done.11) | copy-start | bytes 208900
  66.6 19.9 %collective-permute-start.6 = (bf16[4,32,512]{2,0,1:T(4,128)(2,1)}, bf16[4,32,512]{2,0,1:T(4,128)(2,1)}, u32[]{:S(2)}, u32[]{:S(2)}) collective-permute-start(bf16[4,32,512]{2,0,1:T(4,128)(2,1)} %collective-permute-done.5), channel_id=1, source_target_pairs={{0,8},{8,16},{16,24},{24,0},{1,9},{9,17},{17,25},{25,1},{2,10},{10... | collective-permute-start | bytes 393224 | tf_op jit(solution)/shard_map/ppermute | solution.py:23
  84.6 1.9 %copy-start.4 = (bf16[4,32,512]{2,0,1:T(4,128)(2,1)S(1)}, bf16[4,32,512]{2,0,1:T(4,128)(2,1)}, u32[]{:S(2)}) copy-start(bf16[4,32,512]{2,0,1:T(4,128)(2,1)} %copy-done.3) | copy-start | bytes 393220
  86.5 3.5 %copy-start.9 = (pred[4]{0:T(512)(128)(4,1)S(1)}, pred[4]{0:T(512)(128)(4,1)}, u32[]{:S(2)}) copy-start(pred[4]{0:T(512)(128)(4,1)} %compare_and_fusion.2) | copy-start | bytes 16
  86.5 35.2 %copy-start.2 = (bf16[4,512,512]{2,1,0:T(8,128)(2,1)S(1)}, bf16[4,512,512]{2,1,0:T(8,128)(2,1)}, u32[]{:S(2)}) copy-start(bf16[4,512,512]{2,1,0:T(8,128)(2,1)} %gather_fusion.4) | copy-start | bytes 6291460
  121.7 6.7 %copy-start.10 = (pred[4,4]{1,0:T(4,128)(4,1)S(1)}, pred[4,4]{1,0:T(4,128)(4,1)}, u32[]{:S(2)}) copy-start(pred[4,4]{1,0:T(4,128)(4,1)} %fusion.79) | copy-start | bytes 52
  121.8 6.7 %copy-start.14 = (bf16[4,1,1]{0,2,1:T(2,128)(2,1)S(1)}, bf16[4,1,1]{0,2,1:T(2,128)(2,1)}, u32[]{:S(2)}) copy-start(bf16[4,1,1]{0,2,1:T(2,128)(2,1)} %param.13) | copy-start | bytes 28
  134.2 10.8 %copy-start.15 = (u32[32]{0:T(128)S(1)}, u32[32]{0:T(128)}, u32[]{:S(2)}) copy-start(u32[32]{0:T(128)} %constant.197) | copy-start | bytes 388
Sparse Core Ops, SparseCore 0:
  134.4 43.6 reduce-scatter.1
